TPU v7x, 128 devices: a whole 4x4x4 slice. The times are simulated.
128 devices in a mesh: leaf: 8 (over z, core), expert: 8 (over x_hi, y), tensor: 2 (over x_lo).
Axes of the slice: x: 4 (x_hi: 2, x_lo: 2; x = x_hi * 2 + x_lo), y: 4, z: 4, core: 2. Of those that a mesh axis runs over, the one named last changes fastest.
Arguments:
- drafts: bfloat16 [2048, 6144], P('leaf', ('expert', 'tensor')), may hold values from -6 to 6
- children: bfloat16 [4096, 6144], P('leaf', ('expert', 'tensor')), may hold values from -6 to 6
- child_order: int32 [16], replicated, may hold values from 0 to 15, each once
- spans: int32 [4096], P('leaf'), may hold values from 0 to 15
- span_bias: float32 [48, 16], P(('expert', 'tensor')), may hold values from -4 to 4
- out_weight: bfloat16 [6144, 6144], P(('expert', 'tensor')), may hold values from -0.078125 to 0.078125
- norm_gain: float32 [6144], replicated, may hold values from 0.1 to 1.9
- router: bfloat16 [6144, 8], replicated, may hold values from -0.078125 to 0.078125
- routes: int32 [2048, 2], P(('leaf', 'expert')), may hold values from 0 to 7, all different within a row; in each aligned block of 32 rows (0 to 31, 32 to 63, ...) at most 16 rows name the same one
- w_gate: bfloat16 [8, 6144, 8192], P('expert', None, ('leaf', 'tensor')), may hold values from -0.078125 to 0.078125
- w_up: bfloat16 [8, 6144, 8192], P('expert', None, ('leaf', 'tensor')), may hold values from -0.078125 to 0.078125
- w_down: bfloat16 [8, 8192, 6144], P('expert', ('leaf', 'tensor')), may hold values from -0.0625 to 0.0625
Outputs:
- merged_out: float32 [2048, 6144], P(('leaf', 'expert'))
Inputs may be any that keep to these rules, and one draw needn't show every extreme that they name: `routes`: each row names two different experts; within the rows of one index pair of leaf and expert (32 aligned rows) no expert is named more than 16 times, and exactly 16 times in some of them. `child_order`: A permutation: every parent has exactly two children.
All inputs are finite; a program needn't handle non-finite values.
Results may differ from a plain program's by a relative error of at most 0.013.
Values may be sent and summed in bfloat16 or wider, within the bound.
No kernel may reach another device: no remote copies, remote signals or barrier semaphores. Data moves between devices by JAX's collectives and lax.ppermute only.
A program may use at most 128 MiB of HBM per device.

v0:
```python
import math
import jax
import jax.numpy as jnp
from jax import lax
from jax.sharding import PartitionSpec as P

R = 256


def attend_parent(queries, keys, key_spans, span_bias, scale):
    rows, local_width = queries.shape
    heads_here, span_count = span_bias.shape
    head_size = local_width // heads_here
    key_count = keys.shape[0]
    q = queries.reshape(rows, heads_here, head_size)
    k = keys.reshape(key_count, heads_here, head_size)
    scores = jnp.einsum("qhd,khd->hqk", q, k, preferred_element_type=jnp.float32) * scale
    span_hot = (key_spans[:, None] == jnp.arange(span_count, dtype=jnp.int32)[None, :]).astype(
        jnp.float32
    )
    bias = jnp.dot(span_hot, span_bias.T, precision=lax.Precision.HIGHEST)
    scores = scores + bias.T[:, None, :]
    top = jnp.max(scores, axis=-1, keepdims=True)
    weights = jnp.exp(scores - top)
    total = jnp.sum(weights, axis=-1, keepdims=True)
    high = weights.astype(jnp.bfloat16)
    low = (weights - high.astype(jnp.float32)).astype(jnp.bfloat16)
    values = jnp.einsum("hqk,khd->hqd", high, k, preferred_element_type=jnp.float32) + jnp.einsum(
        "hqk,khd->hqd", low, k, preferred_element_type=jnp.float32
    )
    return (values / total).transpose(1, 0, 2).reshape(rows, local_width).astype(jnp.bfloat16)


def pair_gather(share):
    other = lax.ppermute(share, "tensor", perm=[(0, 1), (1, 0)])
    low = lax.axis_index("tensor") == 0
    return jnp.concatenate([jnp.where(low, share, other), jnp.where(low, other, share)], axis=0)


def per_device(
    drafts,
    children,
    child_order,
    spans,
    span_bias,
    out_weight,
    norm_gain,
    router,
    routes,
    w_gate,
    w_up,
    w_down,
):
    local_rows, local_width = drafts.shape
    heads_here = span_bias.shape[0]
    head_size = local_width // heads_here
    width = out_weight.shape[1]
    scale = 1.0 / math.sqrt(head_size)
    parents_here = local_rows // R
    leaf_index = lax.axis_index("leaf")
    child_rows = children.shape[0]
    children_here = child_rows // R
    span_rows = -(-spans.shape[0] // local_width)
    span_rows = -(-span_rows // 8) * 8
    span_block = jnp.pad(spans.astype(jnp.bfloat16), (0, span_rows * local_width - spans.shape[0]))
    payload = jnp.concatenate([children, span_block.reshape(span_rows, local_width)], axis=0)
    n_leaf = lax.axis_size("leaf")
    n_z = n_leaf // 2
    core = leaf_index % 2
    z = leaf_index // 2
    got = [payload]
    for k in range(1, n_z):
        perm = [(a * 2 + b, (a + k) % n_z * 2 + b) for a in range(n_z) for b in range(2)]
        got.append(lax.ppermute(payload, "leaf", perm=perm))
    swap = [(j, j ^ 1) for j in range(n_leaf)]
    got = got + [lax.ppermute(block, "leaf", perm=swap) for block in got]
    gathered = jnp.stack(got)
    span_table = gathered[:, child_rows:].reshape(gathered.shape[0], span_rows * local_width)
    count = child_order.shape[0]
    ids = jnp.arange(count, dtype=jnp.int32)
    inverse = jnp.sum(jnp.where(child_order[None, :] == ids[:, None], ids[None, :], 0), axis=1)

    def child_keys(child):
        owner = child // children_here
        slot = jnp.where(owner % 2 == core, 0, n_z) + (z - owner // 2) % n_z
        offset = child % children_here * R
        rows = lax.dynamic_slice(gathered, (slot, offset, 0), (1, R, local_width))[0]
        marks = lax.dynamic_slice(span_table, (slot, offset), (1, R))[0]
        return (rows, marks.astype(jnp.int32))

    pieces = []
    for i in range(parents_here):
        parent = leaf_index * parents_here + i
        first_rows, first_spans = child_keys(inverse[2 * parent])
        second_rows, second_spans = child_keys(inverse[2 * parent + 1])
        own_keys = jnp.concatenate([first_rows, second_rows], axis=0)
        own_spans = jnp.concatenate([first_spans, second_spans], axis=0)
        pieces.append(
            attend_parent(drafts[i * R : (i + 1) * R], own_keys, own_spans, span_bias, scale)
        )
    attended = pieces[0] if parents_here == 1 else jnp.concatenate(pieces, axis=0)
    term = jnp.dot(attended, out_weight, preferred_element_type=jnp.float32)
    offset = lax.axis_index(("expert", "tensor")) * local_width
    own_cols = lax.dynamic_slice(term, (0, offset), (local_rows, local_width)) + drafts.astype(
        jnp.float32
    )
    term = lax.dynamic_update_slice(term, own_cols, (0, offset)).astype(jnp.bfloat16)
    group = lax.axis_size(("expert", "tensor"))
    share_rows = local_rows // group
    arrived_terms = lax.all_to_all(
        term.reshape(group, share_rows, width), ("expert", "tensor"), 0, 0, tiled=True
    )
    share = jnp.sum(arrived_terms.astype(jnp.float32), axis=0)
    mean_square = jnp.mean(share * share, axis=-1, keepdims=True)
    normed = pair_gather((share * lax.rsqrt(mean_square + 1e-05) * norm_gain).astype(jnp.bfloat16))
    logits = jnp.dot(normed, router, preferred_element_type=jnp.float32)
    experts = router.shape[1]
    tok_count = routes.shape[0]
    capacity = 4 * tok_count // lax.axis_size("expert")
    choice_hot = routes[:, :, None] == jnp.arange(experts, dtype=jnp.int32)[None, None, :]
    chosen = jnp.sum(jnp.where(choice_hot, logits[:, None, :], 0.0), axis=-1)
    gates = jax.nn.softmax(chosen, axis=-1)
    pairs = routes.reshape(-1)
    pair_hot = (pairs[:, None] == jnp.arange(experts, dtype=jnp.int32)[None, :]).astype(jnp.int32)
    earlier = jnp.cumsum(pair_hot, axis=0) - pair_hot
    slot_index = jnp.sum(earlier * pair_hot, axis=1)
    target = pairs * capacity + slot_index
    place_hot = (
        jnp.arange(experts * capacity, dtype=jnp.int32)[:, None] == target[None, :]
    ).astype(jnp.bfloat16)
    place_rows = jnp.sum(place_hot.reshape(experts * capacity, tok_count, 2), axis=-1)
    outgoing = jnp.dot(place_rows, normed, preferred_element_type=jnp.float32).astype(jnp.bfloat16)
    outgoing = outgoing.reshape(experts, capacity, width)
    chunks = 2
    chunk_slots = capacity // chunks
    returned = []
    for c in range(chunks):
        arrived = lax.all_to_all(
            outgoing[:, c * chunk_slots : (c + 1) * chunk_slots],
            "expert",
            split_axis=0,
            concat_axis=0,
            tiled=True,
        ).reshape(-1, width)
        piece = lax.all_gather(arrived, "leaf", axis=0, tiled=True)
        if c == 0:
            piece, share = lax.optimization_barrier((piece, share))
            other_share = lax.ppermute(share, "tensor", perm=[(0, 1), (1, 0)])
        else:
            piece, other_share = lax.optimization_barrier((piece, other_share))
        gate_v = jnp.dot(piece, w_gate[0], preferred_element_type=jnp.float32)
        up_v = jnp.dot(piece, w_up[0], preferred_element_type=jnp.float32)
        hidden = (jax.nn.silu(gate_v) * up_v).astype(jnp.bfloat16)
        down = jnp.dot(hidden, w_down[0], preferred_element_type=jnp.float32).astype(jnp.bfloat16)
        part_rows = lax.psum_scatter(down, "leaf", scatter_dimension=0, tiled=True)
        returned.append(
            lax.all_to_all(
                part_rows.reshape(experts, chunk_slots, width),
                "expert",
                split_axis=0,
                concat_axis=0,
                tiled=True,
            )
        )
    back = jnp.concatenate(returned, axis=1).reshape(-1, width)
    low = lax.axis_index("tensor") == 0
    merged = jnp.concatenate(
        [jnp.where(low, share, other_share), jnp.where(low, other_share, share)], axis=0
    )
    picked = jnp.take(back, target, axis=0)
    picked = picked.astype(jnp.float32).reshape(tok_count, 2, width)
    own_mix = (gates[:, 0:1] * picked[:, 0] + gates[:, 1:2] * picked[:, 1]).astype(jnp.bfloat16)
    other_mix = lax.ppermute(own_mix, "tensor", perm=[(0, 1), (1, 0)])
    mixed = own_mix.astype(jnp.float32) + other_mix.astype(jnp.float32)
    return merged + mixed


def solution(mesh):
    in_specs = (
        P("leaf", ("expert", "tensor")),
        P("leaf", ("expert", "tensor")),
        P(),
        P("leaf"),
        P(("expert", "tensor"), None),
        P(("expert", "tensor"), None),
        P(),
        P(),
        P(("leaf", "expert"), None),
        P("expert", None, ("leaf", "tensor")),
        P("expert", None, ("leaf", "tensor")),
        P("expert", ("leaf", "tensor"), None),
    )
    out_specs = P(("leaf", "expert"), None)
    return jax.shard_map(
        per_device, mesh=mesh, in_specs=in_specs, out_specs=out_specs, check_vma=False
    )
```

profile of v0, /device:TPU:32, one launch (start us, length us, event | category | flops | bytes accessed | tf_op | source)
XLA Modules:
  0.0 337.6 jit_solution(6291394186603698562)
XLA Ops:
  11.8 2.5 collective-permute-start.2
  21.9 9.8 %collective-permute-done = bf16[520,384]{0,1:T(8,128)(2,1)S(1)} collective-permute-done((bf16[520,384]{0,1:T(8,128)(2,1)S(1)}, bf16[520,384]{0,1:T(8,128)(2,1)S(1)}, u32[]{:S(2)}, u32[]{:S(2)}) %collective-permute-start) | collective-permute-done | bytes 399392 | tf_op jit(solution)/shard_map/ppermute | solution.py:74
  32.3 2.7 collective-permute-done.2
  42.9 2.1 convert_element_type.89
  45.0 7.2 %all-to-all-start = ((bf16[16,16,6144]{2,1,0:T(8,128)(2,1)}), bf16[16,16,6144]{2,1,0:T(8,128)(2,1)S(1)}, u32[]{:S(2)}, u32[]{:S(2)}) async-start(bf16[16,16,6144]{2,1,0:T(8,128)(2,1)} %bitcast.114), calls=%async_computation | async-start | bytes 6291456 | tf_op jit(solution)/shard_map/all_to_all | solution.py:110
  52.9 45.7 %all-to-all-done = bf16[16,16,6144]{2,1,0:T(8,128)(2,1)S(1)} async-done(((bf16[16,16,6144]{2,1,0:T(8,128)(2,1)}), bf16[16,16,6144]{2,1,0:T(8,128)(2,1)S(1)}, u32[]{:S(2)}, u32[]{:S(2)}) %all-to-all-start) | async-done | bytes 3145760 | tf_op jit(solution)/shard_map/all_to_all | solution.py:110
  100.0 2.8 collective-permute-start.7
  102.8 4.0 %collective-permute-done.7 = bf16[16,6144]{1,0:T(8,128)(2,1)S(1)} collective-permute-done((bf16[16,6144]{1,0:T(8,128)(2,1)S(1)}, bf16[16,6144]{1,0:T(8,128)(2,1)S(1)}, u32[]{:S(2)}, u32[]{:S(2)}) %collective-permute-start.7) | collective-permute-done | bytes 196640 | tf_op jit(solution)/shard_map/ppermute | solution.py:35
  108.7 17.8 %all_to_all.25 = bf16[8,8,6144]{2,1,0:T(8,128)(2,1)} all-to-all(bf16[8,8,6144]{2,1,0:T(8,128)(2,1)S(1)} %get-tuple-element.19), channel_id=1, replica_groups=mesh['leaf'=8,'expert'=8,'tensor'=2] {'expert'}, dimensions={0} | all-to-all | bytes 1572864 | tf_op jit(solution)/shard_map/all_to_all | solution.py:138
  126.6 14.6 %all_to_all.26 = bf16[8,8,6144]{2,1,0:T(8,128)(2,1)} all-to-all(bf16[8,8,6144]{2,1,0:T(8,128)(2,1)S(1)} %get-tuple-element.20), channel_id=1, replica_groups=mesh['leaf'=8,'expert'=8,'tensor'=2] {'expert'}, dimensions={0} | all-to-all | bytes 1572864 | tf_op jit(solution)/shard_map/all_to_all | solution.py:138
  141.5 22.4 %all-gather.3.cloned.1.call-done = bf16[512,6144]{1,0:T(8,128)(2,1)} async-done(((bf16[64,6144]{1,0:T(8,128)(2,1)}), bf16[512,6144]{1,0:T(8,128)(2,1)}) %all-gather.3.cloned.1.call-update) | async-done | bytes 6291472 | tf_op jit(solution)/shard_map/all_gather | solution.py:145
  163.9 8.2 %fusion.8 = f32[512,512]{1,0:T(8,128)S(1)} fusion(bf16[512,6144]{1,0:T(8,128)(2,1)} %all-gather.3.cloned.1.call-done, bf16[1,6144,512]{2,1,0:T(8,128)(2,1)} %param.21), kind=kOutput, calls=%fused_computation.12 | convolution fusion | flops 3221225472 | bytes 13631488 | tf_op jit(solution)/shard_map/dot_general | solution.py:151
  172.2 6.4 %fusion.14 = bf16[512,512]{1,0:T(8,128)(2,1)S(1)} fusion(bf16[512,6144]{1,0:T(8,128)(2,1)S(1)} %copy-done.7, bf16[1,6144,512]{2,1,0:T(8,128)(2,1)} %param.22, f32[512,512]{1,0:T(8,128)S(1)} %fusion.8), kind=kOutput, calls=%fused_computation.22 | convolution fusion | flops 3222798336 | bytes 14155776 | tf_op jit(solution)/shard_map/dot_general | solution.py:152
  178.7 5.4 %convolution_convert_fusion.1 = bf16[512,6144]{1,0:T(8,128)(2,1)} fusion(bf16[512,512]{1,0:T(8,128)(2,1)S(1)} %fusion.14, bf16[1,512,6144]{2,1,0:T(8,128)(2,1)S(1)} %bitcast.130), kind=kOutput, calls=%fused_computation.2 | convolution fusion | flops 3224371200 | bytes 13107200 | tf_op jit(solution)/shard_map/dot_general | solution.py:154
  186.5 20.2 %all-gather.5.cloned.1.call-done = bf16[512,6144]{1,0:T(8,128)(2,1)} async-done(((bf16[64,6144]{1,0:T(8,128)(2,1)}), bf16[512,6144]{1,0:T(8,128)(2,1)}) %all-gather.5.cloned.1.call-update) | async-done | bytes 6291472 | tf_op jit(solution)/shard_map/all_gather | solution.py:145
  206.7 7.6 %fusion.2 = f32[512,512]{1,0:T(8,128)S(1)} fusion(bf16[512,6144]{1,0:T(8,128)(2,1)} %all-gather.5.cloned.1.call-done, bf16[1,6144,512]{2,1,0:T(8,128)(2,1)} %param.22), kind=kOutput, calls=%fused_computation.6 | convolution fusion | flops 3221225472 | bytes 13631488 | tf_op jit(solution)/shard_map/dot_general | solution.py:152
  214.3 5.7 %fusion.6 = f32[512,512]{1,0:T(8,128)S(1)} fusion(bf16[512,6144]{1,0:T(8,128)(2,1)S(1)} %copy-done.6, bf16[1,6144,512]{2,1,0:T(8,128)(2,1)} %param.21), kind=kOutput, calls=%fused_computation.10 | convolution fusion | flops 3221225472 | bytes 13631488 | tf_op jit(solution)/shard_map/dot_general | solution.py:151
  220.1 5.4 %convolution_convert_fusion = bf16[512,6144]{1,0:T(8,128)(2,1)} fusion(bf16[1,512,6144]{2,1,0:T(8,128)(2,1)S(1)} %bitcast.132, f32[512,512]{1,0:T(8,128)S(1)} %fusion.2, f32[512,512]{1,0:T(8,128)S(1)} %fusion.6), kind=kOutput, calls=%fused_computation.1 | convolution fusion | flops 3225944064 | bytes 14680064 | tf_op jit(solution)/shard_map/dot_general | solution.py:154
  225.5 25.0 %reduce-scatter.3.cloned.1.call-done = bf16[64,6144]{1,0:T(8,128)(2,1)} async-done(((bf16[512,6144]{1,0:T(8,128)(2,1)}), bf16[64,6144]{1,0:T(8,128)(2,1)}) %reduce-scatter.3.cloned.1.call-update) | async-done | bytes 786448 | tf_op jit(solution)/shard_map/reduce_scatter | solution.py:155
  250.5 6.7 %all-to-all-start.3 = ((bf16[8,8,6144]{2,1,0:T(8,128)(2,1)}), bf16[8,8,6144]{2,1,0:T(8,128)(2,1)S(1)}, u32[]{:S(2)}, u32[]{:S(2)}) async-start(bf16[8,8,6144]{2,1,0:T(8,128)(2,1)} %bitcast.121), calls=%async_computation.4 | async-start | bytes 1572864 | tf_op jit(solution)/shard_map/all_to_all | solution.py:157
  257.4 37.6 %reduce-scatter.5.cloned.1.call-done = bf16[64,6144]{1,0:T(8,128)(2,1)} async-done(((bf16[512,6144]{1,0:T(8,128)(2,1)}), bf16[64,6144]{1,0:T(8,128)(2,1)}) %reduce-scatter.5.cloned.1.call-update) | async-done | bytes 786448 | tf_op jit(solution)/shard_map/reduce_scatter | solution.py:155
  295.1 6.7 %all-to-all-start.4 = ((bf16[8,8,6144]{2,1,0:T(8,128)(2,1)}), bf16[8,8,6144]{2,1,0:T(8,128)(2,1)}, u32[]{:S(2)}, u32[]{:S(2)}) async-start(bf16[8,8,6144]{2,1,0:T(8,128)(2,1)} %bitcast.122), calls=%async_computation.6 | async-start | bytes 1572864 | tf_op jit(solution)/shard_map/all_to_all | solution.py:157
  302.1 13.6 %all-to-all-done.4 = bf16[8,8,6144]{2,1,0:T(8,128)(2,1)} async-done(((bf16[8,8,6144]{2,1,0:T(8,128)(2,1)}), bf16[8,8,6144]{2,1,0:T(8,128)(2,1)}, u32[]{:S(2)}, u32[]{:S(2)}) %all-to-all-start.4) | async-done | bytes 786464 | tf_op jit(solution)/shard_map/all_to_all | solution.py:157
  320.3 9.6 %collective-permute-done.9 = bf16[32,6144]{1,0:T(8,128)(2,1)S(1)} collective-permute-done((bf16[32,6144]{1,0:T(8,128)(2,1)S(1)}, bf16[32,6144]{1,0:T(8,128)(2,1)S(1)}, u32[]{:S(2)}, u32[]{:S(2)}) %collective-permute-start.9) | collective-permute-done | bytes 393248 | tf_op jit(solution)/shard_map/ppermute | solution.py:173
  (122 shorter events, 29.0 us)
Async XLA Ops:
  6.5 295.3 %copy-start = (bf16[6144,8]{0,1:T(8,128)(2,1)S(1)}, bf16[6144,8]{0,1:T(8,128)(2,1)}, u32[]{:S(2)}) copy-start(bf16[6144,8]{0,1:T(8,128)(2,1)} %param.19) | copy-start | bytes 294916
  8.7 23.0 %collective-permute-start = (bf16[520,384]{0,1:T(8,128)(2,1)S(1)}, bf16[520,384]{0,1:T(8,128)(2,1)S(1)}, u32[]{:S(2)}, u32[]{:S(2)}) collective-permute-start(bf16[520,384]{0,1:T(8,128)(2,1)S(1)} %pad_maximum_fusion.1), channel_id=1, source_target_pairs={{0,32},{16,48},{32,64},{48,80},{64,96},{80,112},{96,0},{112,16},{1... | collective-permute-start | bytes 1198088 | tf_op jit(solution)/shard_map/ppermute | solution.py:74
  10.7 21.1 %collective-permute-start.1 = (bf16[520,384]{0,1:T(8,128)(2,1)S(1)}, bf16[520,384]{0,1:T(8,128)(2,1)S(1)}, u32[]{:S(2)}, u32[]{:S(2)}) collective-permute-start(bf16[520,384]{0,1:T(8,128)(2,1)S(1)} %pad_maximum_fusion.1), channel_id=1, source_target_pairs={{0,64},{16,80},{32,96},{48,112},{64,0},{80,16},{96,32},{112,48},{1... | collective-permute-start | bytes 1198088 | tf_op jit(solution)/shard_map/ppermute | solution.py:74
  11.8 23.2 %collective-permute-start.2 = (bf16[520,384]{0,1:T(8,128)(2,1)S(1)}, bf16[520,384]{0,1:T(8,128)(2,1)S(1)}, u32[]{:S(2)}, u32[]{:S(2)}) collective-permute-start(bf16[520,384]{0,1:T(8,128)(2,1)S(1)} %pad_maximum_fusion.1), channel_id=1, source_target_pairs={{0,96},{16,112},{32,0},{48,16},{64,32},{80,48},{96,64},{112,80},{1... | collective-permute-start | bytes 1198088 | tf_op jit(solution)/shard_map/ppermute | solution.py:74
  14.3 20.8 %collective-permute-start.3 = (bf16[520,384]{0,1:T(8,128)(2,1)S(1)}, bf16[520,384]{0,1:T(8,128)(2,1)S(1)}, u32[]{:S(2)}, u32[]{:S(2)}) collective-permute-start(bf16[520,384]{0,1:T(8,128)(2,1)S(1)} %pad_maximum_fusion.1), channel_id=1, source_target_pairs={{0,16},{16,0},{32,48},{48,32},{64,80},{80,64},{96,112},{112,96},{1... | collective-permute-start | bytes 1198088 | tf_op jit(solution)/shard_map/ppermute | solution.py:76
  31.7 3.6 %collective-permute-start.4 = (bf16[520,384]{0,1:T(8,128)(2,1)S(1)}, bf16[520,384]{0,1:T(8,128)(2,1)S(1)}, u32[]{:S(2)}, u32[]{:S(2)}) collective-permute-start(bf16[520,384]{0,1:T(8,128)(2,1)S(1)} %collective-permute-done), channel_id=1, source_target_pairs={{0,16},{16,0},{32,48},{48,32},{64,80},{80,64},{96,112},{112,96},{1... | collective-permute-start | bytes 1198088 | tf_op jit(solution)/shard_map/ppermute | solution.py:76
  31.7 3.6 %collective-permute-start.5 = (bf16[520,384]{0,1:T(8,128)(2,1)S(1)}, bf16[520,384]{0,1:T(8,128)(2,1)S(1)}, u32[]{:S(2)}, u32[]{:S(2)}) collective-permute-start(bf16[520,384]{0,1:T(8,128)(2,1)S(1)} %collective-permute-done.1), channel_id=1, source_target_pairs={{0,16},{16,0},{32,48},{48,32},{64,80},{80,64},{96,112},{112,96},{1... | collective-permute-start | bytes 1198088 | tf_op jit(solution)/shard_map/ppermute | solution.py:76
  35.0 1.9 collective-permute-start.6
  45.0 7.2 %copy-start.5 = (s32[32,2]{0,1:T(2,128)S(1)}, s32[32,2]{0,1:T(2,128)}, u32[]{:S(2)}) copy-start(s32[32,2]{0,1:T(2,128)} %param.20) | copy-start | bytes 772
  45.0 54.9 %copy-start.4 = (f32[6144]{0:T(1024)S(1)}, f32[6144]{0:T(1024)}, u32[]{:S(2)}) copy-start(f32[6144]{0:T(1024)} %param.18) | copy-start | bytes 73732
  45.0 53.7 %all-to-all-start = ((bf16[16,16,6144]{2,1,0:T(8,128)(2,1)}), bf16[16,16,6144]{2,1,0:T(8,128)(2,1)S(1)}, u32[]{:S(2)}, u32[]{:S(2)}) async-start(bf16[16,16,6144]{2,1,0:T(8,128)(2,1)} %bitcast.114), calls=%async_computation | async-start | bytes 6291456 | tf_op jit(solution)/shard_map/all_to_all | solution.py:110
  52.1 111.8 %all-gather.3.cloned.1.call-start = ((), (), s32[]{:S(2)}) async-start(), calls=%async_computation.7 | async-start | bytes 7077888 | tf_op jit(solution)/shard_map/all_gather | solution.py:145
  100.0 6.9 %collective-permute-start.7 = (bf16[16,6144]{1,0:T(8,128)(2,1)S(1)}, bf16[16,6144]{1,0:T(8,128)(2,1)S(1)}, u32[]{:S(2)}, u32[]{:S(2)}) collective-permute-start(bf16[16,6144]{1,0:T(8,128)(2,1)S(1)} %multiply_convert_fusion.2), channel_id=1, source_target_pairs={{0,1},{1,0},{2,3},{3,2},{4,5},{5,4},{6,7},{7,6},{8,9},{9,8},{10,11... | collective-permute-start | bytes 589832 | tf_op jit(solution)/shard_map/ppermute | solution.py:35
  126.6 80.1 %all-gather.5.cloned.1.call-start = ((), (), s32[]{:S(2)}) async-start(), calls=%async_computation.8 | async-start | bytes 7077888 | tf_op jit(solution)/shard_map/all_gather | solution.py:145
  141.3 109.2 %reduce-scatter.3.cloned.1.call-start = ((), (), s32[]{:S(2)}) async-start(), calls=%async_computation.9 | async-start | bytes 7077888 | tf_op jit(solution)/shard_map/reduce_scatter | solution.py:155
  163.9 8.3 %copy-start.7 = (bf16[512,6144]{1,0:T(8,128)(2,1)S(1)}, bf16[512,6144]{1,0:T(8,128)(2,1)}, u32[]{:S(2)}) copy-start(bf16[512,6144]{1,0:T(8,128)(2,1)} %all-gather.3.cloned.1.call-done) | copy-start | bytes 18874372
  163.9 14.7 %slice-start.2 = ((s8[6291456]{0:T(1024)(128)(4,1)}), s8[4194304]{0:T(1024)(128)(4,1)S(1)}, s32[]{:S(2)}) async-start(s8[6291456]{0:T(1024)(128)(4,1)} %bitcast.129), calls=%async_computation.13 | async-start | bytes 8388608
  184.1 111.0 %reduce-scatter.5.cloned.1.call-start = ((), (), s32[]{:S(2)}) async-start(), calls=%async_computation.10 | async-start | bytes 7077888 | tf_op jit(solution)/shard_map/reduce_scatter | solution.py:155
  185.1 21.6 %collective-permute-start.8 = (f32[16,6144]{1,0:T(8,128)S(1)}, f32[16,6144]{1,0:T(8,128)S(1)}, u32[]{:S(2)}, u32[]{:S(2)}) collective-permute-start(f32[16,6144]{1,0:T(8,128)S(1)} %copy-done.2), channel_id=1, source_target_pairs={{0,1},{1,0},{2,3},{3,2},{4,5},{5,4},{6,7},{7,6},{8,9},{9,8},{10,11... | collective-permute-start | bytes 1179656 | tf_op jit(solution)/shard_map/ppermute | solution.py:148
  206.7 7.6 %copy-start.6 = (bf16[512,6144]{1,0:T(8,128)(2,1)S(1)}, bf16[512,6144]{1,0:T(8,128)(2,1)}, u32[]{:S(2)}) copy-start(bf16[512,6144]{1,0:T(8,128)(2,1)} %all-gather.5.cloned.1.call-done) | copy-start | bytes 18874372
  206.7 13.4 %slice-start.4 = ((s8[6291456]{0:T(1024)(128)(4,1)}), s8[4194304]{0:T(1024)(128)(4,1)S(1)}, s32[]{:S(2)}) async-start(s8[6291456]{0:T(1024)(128)(4,1)} %bitcast.131), calls=%async_computation.15 | async-start | bytes 8388608
  250.5 44.6 %all-to-all-start.3 = ((bf16[8,8,6144]{2,1,0:T(8,128)(2,1)}), bf16[8,8,6144]{2,1,0:T(8,128)(2,1)S(1)}, u32[]{:S(2)}, u32[]{:S(2)}) async-start(bf16[8,8,6144]{2,1,0:T(8,128)(2,1)} %bitcast.121), calls=%async_computation.4 | async-start | bytes 1572864 | tf_op jit(solution)/shard_map/all_to_all | solution.py:157
  295.1 20.7 %all-to-all-start.4 = ((bf16[8,8,6144]{2,1,0:T(8,128)(2,1)}), bf16[8,8,6144]{2,1,0:T(8,128)(2,1)}, u32[]{:S(2)}, u32[]{:S(2)}) async-start(bf16[8,8,6144]{2,1,0:T(8,128)(2,1)} %bitcast.122), calls=%async_computation.6 | async-start | bytes 1572864 | tf_op jit(solution)/shard_map/all_to_all | solution.py:157
  319.2 10.8 %collective-permute-start.9 = (bf16[32,6144]{1,0:T(8,128)(2,1)S(1)}, bf16[32,6144]{1,0:T(8,128)(2,1)S(1)}, u32[]{:S(2)}, u32[]{:S(2)}) collective-permute-start(bf16[32,6144]{1,0:T(8,128)(2,1)S(1)} %fusion.26), channel_id=1, source_target_pairs={{0,1},{1,0},{2,3},{3,2},{4,5},{5,4},{6,7},{7,6},{8,9},{9,8},{10,11... | collective-permute-start | bytes 1179656 | tf_op jit(solution)/shard_map/ppermute | solution.py:173
  (8 other events, 23.7 us)
Sparse Core Ops, SparseCore 0:
  126.7 37.2 all-gather.2
  165.6 41.0 all-gather.4
  209.1 41.3 reduce-scatter.2
  252.8 42.2 reduce-scatter.4
where the time goes:
time: 338 us
  waiting for transfers between devices  192 us (57%)
  matrix products  43 us (13%)
  blocking collectives  32.5 us (10%)
  starting transfers between devices  32.4 us (10%)
  between operations  18.6 us (6%)
  other arithmetic  9.42 us (3%)
  local copies, waits for them, and re-layouts  9.3 us (3%)
    reduce_scatter x2, waiting for transfers between devices, per_device(): part_rows = lax.psum_scatter(down, 'leaf', scatter_dimension=0, tiled=True)  62.6 us
    all_to_all x1, waiting for transfers between devices, per_device(): lax.all_to_all(term.reshape(group, share_rows, width), ('expert', 'tensor...  45.7 us
    all_gather x2, waiting for transfers between devices, per_device(): piece = lax.all_gather(arrived, 'leaf', axis=0, tiled=True)  42.6 us
    all_to_all x2, blocking collectives, per_device(): lax.all_to_all(outgoing[:, c * chunk_slots:(c + 1) * chunk_slots], 'exper...  32.5 us
    dot_general x2, matrix products, per_device(): up_v = jnp.dot(piece, w_up[0], preferred_element_type=jnp.float32)  14 us
    dot_general x2, matrix products, per_device(): gate_v = jnp.dot(piece, w_gate[0], preferred_element_type=jnp.float32)  14 us
    all_to_all x2, waiting for transfers between devices, per_device(): lax.all_to_all(part_rows.reshape(experts, chunk_slots, width), 'expert',...  13.6 us
    all_to_all x2, starting transfers between devices, per_device(): lax.all_to_all(part_rows.reshape(experts, chunk_slots, width), 'expert',...  13.4 us
  transfers between devices with their start and end apart: 17, of which 11 were waited for; matrix products, arithmetic and copies ran while one was open for 13% of the time, Pallas kernels for 0%

commit v1 on v0

--- a/solution.py
+++ b/solution.py
@@ -142,7 +142,16 @@
             concat_axis=0,
             tiled=True,
         ).reshape(-1, width)
-        piece = lax.all_gather(arrived, "leaf", axis=0, tiled=True)
+        ways = lax.axis_size("leaf")
+        up = [(d, (d + 1) % ways) for d in range(ways)]
+        down_2 = [(d, (d - 1) % ways) for d in range(ways)]
+        earlier_2, later = ([arrived], [arrived])
+        for _ in range(ways // 2):
+            earlier_2.append(lax.ppermute(earlier_2[-1], "leaf", up))
+        for _ in range((ways - 1) // 2):
+            later.append(lax.ppermute(later[-1], "leaf", down_2))
+        line = jnp.concatenate([*earlier_2[::-1], *later[1:]], axis=0)
+        piece = jnp.roll(line, (lax.axis_index("leaf") - ways // 2) * arrived.shape[0], axis=0)
         if c == 0:
             piece, share = lax.optimization_barrier((piece, share))
             other_share = lax.ppermute(share, "tensor", perm=[(0, 1), (1, 0)])

time: 338 us -> 373 us (1.10)
  waiting for transfers between devices: 192 us -> 209 us
  matrix products: 43 us -> 28.6 us
  other arithmetic: 9.42 us -> 22.8 us
  local copies, waits for them, and re-layouts: 9.3 us -> 17.4 us
  starting transfers between devices: 32.4 us -> 39.3 us
    ppermute x0 -> x14, waiting for transfers between devices: none -> 82.5 us  [the longest x8 42.7 us: per_device(): earlier_2.append(lax.ppermute(earlier_2[-1], 'leaf', up))]
    all_gather x2 -> x0, waiting for transfers between devices: 42.6 us -> none  [per_device(): piece = lax.all_gather(arrived, 'leaf', axis=0, tiled=True)]
    reduce_scatter x2, waiting for transfers between devices: 62.6 us -> 39.3 us  [per_device(): part_rows = lax.psum_scatter(down, 'leaf', scatter_dimension=0, tiled=True)]
    concatenate x0 -> x2, other arithmetic: none -> 13.4 us  [per_device(): jnp.roll(line, (lax.axis_index('leaf') - ways // 2) * arrived.shape[0], a...]
    ppermute x0 -> x14, starting transfers between devices: none -> 10.7 us  [the longest x6 10.2 us: per_device(): later.append(lax.ppermute(later[-1], 'leaf', down_2))]
    unnamed x40 -> x74, local copies, waits for them, and re-layouts: 5.32 us -> 13.3 us
    dot_general x2, matrix products: 14 us -> 6.8 us  [per_device(): gate_v = jnp.dot(piece, w_gate[0], preferred_element_type=jnp.float32)]
    dot_general x2, matrix products: 14 us -> 6.88 us  [per_device(): up_v = jnp.dot(piece, w_up[0], preferred_element_type=jnp.float32)]
  transfers between devices with their start and end apart: 17 -> 29, of which waited for: 11 -> 18; matrix products, arithmetic and copies ran while one was open for 13% -> 14% of each run, Pallas kernels for 0% -> 0%
where the time goes in v1:
time: 373 us; the launch traced here: 372 us
  waiting for transfers between devices  209 us (56%)
  starting transfers between devices  39.3 us (11%)
  blocking collectives  35.7 us (10%)
  matrix products  28.6 us (8%)
  other arithmetic  22.8 us (6%)
  between operations  19.5 us (5%)
  local copies, waits for them, and re-layouts  17.4 us (5%)
    all_to_all x1, waiting for transfers between devices, per_device(): lax.all_to_all(term.reshape(group, share_rows, width), ('expert', 'tensor...  45.7 us
    ppermute x8, waiting for transfers between devices, per_device(): earlier_2.append(lax.ppermute(earlier_2[-1], 'leaf', up))  42.7 us
    ppermute x6, waiting for transfers between devices, per_device(): later.append(lax.ppermute(later[-1], 'leaf', down_2))  39.8 us
    reduce_scatter x2, waiting for transfers between devices, per_device(): part_rows = lax.psum_scatter(down, 'leaf', scatter_dimension=0, tiled=True)  39.3 us
    all_to_all x2, blocking collectives, per_device(): lax.all_to_all(outgoing[:, c * chunk_slots:(c + 1) * chunk_slots], 'exper...  35.7 us
    all_to_all x2, waiting for transfers between devices, per_device(): lax.all_to_all(part_rows.reshape(experts, chunk_slots, width), 'expert',...  13.6 us
    concatenate x2, other arithmetic, per_device(): jnp.roll(line, (lax.axis_index('leaf') - ways // 2) * arrived.shape[0], a...  13.4 us
    unnamed x74, local copies, waits for them, and re-layouts  13.3 us
  transfers between devices with their start and end apart: 29, of which 18 were waited for; matrix products, arithmetic and copies ran while one was open for 14% of the time, Pallas kernels for 0%

profile of v1, /device:TPU:32, one launch (start us, length us, event | category | flops | bytes accessed | tf_op | source)
XLA Modules:
  0.0 371.9 jit_solution(15548831588236027359)
XLA Ops:
  22.1 9.6 %collective-permute-done = bf16[520,384]{0,1:T(8,128)(2,1)S(1)} collective-permute-done((bf16[520,384]{0,1:T(8,128)(2,1)S(1)}, bf16[520,384]{0,1:T(8,128)(2,1)S(1)}, u32[]{:S(2)}, u32[]{:S(2)}) %collective-permute-start) | collective-permute-done | bytes 399392 | tf_op jit(solution)/shard_map/ppermute | solution.py:74
  45.0 7.2 %all-to-all-start = ((bf16[16,16,6144]{2,1,0:T(8,128)(2,1)}), bf16[16,16,6144]{2,1,0:T(8,128)(2,1)S(1)}, u32[]{:S(2)}, u32[]{:S(2)}) async-start(bf16[16,16,6144]{2,1,0:T(8,128)(2,1)} %bitcast.116), calls=%async_computation | async-start | bytes 6291456 | tf_op jit(solution)/shard_map/all_to_all | solution.py:110
  52.9 45.7 %all-to-all-done = bf16[16,16,6144]{2,1,0:T(8,128)(2,1)S(1)} async-done(((bf16[16,16,6144]{2,1,0:T(8,128)(2,1)}), bf16[16,16,6144]{2,1,0:T(8,128)(2,1)S(1)}, u32[]{:S(2)}, u32[]{:S(2)}) %all-to-all-start) | async-done | bytes 3145760 | tf_op jit(solution)/shard_map/all_to_all | solution.py:110
  102.8 4.0 %collective-permute-done.7 = bf16[16,6144]{1,0:T(8,128)(2,1)S(1)} collective-permute-done((bf16[16,6144]{1,0:T(8,128)(2,1)S(1)}, bf16[16,6144]{1,0:T(8,128)(2,1)S(1)}, u32[]{:S(2)}, u32[]{:S(2)}) %collective-permute-start.7) | collective-permute-done | bytes 196640 | tf_op jit(solution)/shard_map/ppermute | solution.py:35
  108.7 17.7 %all_to_all.25 = bf16[8,8,6144]{2,1,0:T(8,128)(2,1)S(1)} all-to-all(bf16[8,8,6144]{2,1,0:T(8,128)(2,1)S(1)} %get-tuple-element.20), channel_id=1, replica_groups=mesh['leaf'=8,'expert'=8,'tensor'=2] {'expert'}, dimensions={0} | all-to-all | bytes 1572864 | tf_op jit(solution)/shard_map/all_to_all | solution.py:138
  126.4 11.4 %collective-permute-done.8 = bf16[64,6144]{1,0:T(8,128)(2,1)S(1)} collective-permute-done((bf16[64,6144]{1,0:T(8,128)(2,1)S(1)}, bf16[64,6144]{1,0:T(8,128)(2,1)S(1)}, u32[]{:S(2)}, u32[]{:S(2)}) %collective-permute-start.8) | collective-permute-done | bytes 786464 | tf_op jit(solution)/shard_map/ppermute | solution.py:150
  139.6 9.7 %collective-permute-done.9 = bf16[64,6144]{1,0:T(8,128)(2,1)S(1)} collective-permute-done((bf16[64,6144]{1,0:T(8,128)(2,1)S(1)}, bf16[64,6144]{1,0:T(8,128)(2,1)S(1)}, u32[]{:S(2)}, u32[]{:S(2)}) %collective-permute-start.9) | collective-permute-done | bytes 786464 | tf_op jit(solution)/shard_map/ppermute | solution.py:150
  149.3 18.0 %all_to_all.26 = bf16[8,8,6144]{2,1,0:T(8,128)(2,1)S(1)} all-to-all(bf16[8,8,6144]{2,1,0:T(8,128)(2,1)S(1)} %get-tuple-element.21), channel_id=1, replica_groups=mesh['leaf'=8,'expert'=8,'tensor'=2] {'expert'}, dimensions={0} | all-to-all | bytes 1572864 | tf_op jit(solution)/shard_map/all_to_all | solution.py:138
  169.0 9.6 %collective-permute-done.15 = bf16[64,6144]{1,0:T(8,128)(2,1)S(1)} collective-permute-done((bf16[64,6144]{1,0:T(8,128)(2,1)S(1)}, bf16[64,6144]{1,0:T(8,128)(2,1)S(1)}, u32[]{:S(2)}, u32[]{:S(2)}) %collective-permute-start.15) | collective-permute-done | bytes 786464 | tf_op jit(solution)/shard_map/ppermute | solution.py:150
  180.9 6.3 %collective-permute-done.11 = bf16[64,6144]{1,0:T(8,128)(2,1)} collective-permute-done((bf16[64,6144]{1,0:T(8,128)(2,1)}, bf16[64,6144]{1,0:T(8,128)(2,1)}, u32[]{:S(2)}, u32[]{:S(2)}) %collective-permute-start.11) | collective-permute-done | bytes 786464 | tf_op jit(solution)/shard_map/ppermute | solution.py:150
  194.6 6.7 %fusion.1 = bf16[512,6144]{1,0:T(8,128)(2,1)S(1)} fusion(s32[]{:T(128)S(6)} %select_n.181, bf16[512,6144]{1,0:T(8,128)(2,1)S(1)} %constant_dynamic-update-slice_fusion), kind=kLoop, calls=%fused_computation.9 | loop fusion | flops 12582912 | bytes 12582916 | tf_op jit(solution)/shard_map/jit(_roll_dynamic)/concatenate | solution.py:154
  204.8 3.5 fusion.16
  208.3 5.4 %convolution_convert_fusion.1 = bf16[512,6144]{1,0:T(8,128)(2,1)} fusion(bf16[512,512]{1,0:T(8,128)(2,1)S(1)} %fusion.16, bf16[1,512,6144]{2,1,0:T(8,128)(2,1)S(1)} %bitcast.142), kind=kOutput, calls=%fused_computation.6 | convolution fusion | flops 3224371200 | bytes 13107200 | tf_op jit(solution)/shard_map/dot_general | solution.py:163
  214.3 11.9 %collective-permute-done.19 = bf16[64,6144]{1,0:T(8,128)(2,1)S(1)} collective-permute-done((bf16[64,6144]{1,0:T(8,128)(2,1)S(1)}, bf16[64,6144]{1,0:T(8,128)(2,1)S(1)}, u32[]{:S(2)}, u32[]{:S(2)}) %collective-permute-start.19) | collective-permute-done | bytes 786464 | tf_op jit(solution)/shard_map/ppermute | solution.py:152
  228.5 3.6 collective-permute-done.17
  232.1 14.5 %collective-permute-done.20 = bf16[64,6144]{1,0:T(8,128)(2,1)S(1)} collective-permute-done((bf16[64,6144]{1,0:T(8,128)(2,1)S(1)}, bf16[64,6144]{1,0:T(8,128)(2,1)S(1)}, u32[]{:S(2)}, u32[]{:S(2)}) %collective-permute-start.20) | collective-permute-done | bytes 786464 | tf_op jit(solution)/shard_map/ppermute | solution.py:152
  253.6 13.3 %collective-permute-done.21 = bf16[64,6144]{1,0:T(8,128)(2,1)S(1)} collective-permute-done((bf16[64,6144]{1,0:T(8,128)(2,1)S(1)}, bf16[64,6144]{1,0:T(8,128)(2,1)S(1)}, u32[]{:S(2)}, u32[]{:S(2)}) %collective-permute-start.21) | collective-permute-done | bytes 786464 | tf_op jit(solution)/shard_map/ppermute | solution.py:152
  267.0 6.7 %fusion = bf16[512,6144]{1,0:T(8,128)(2,1)S(1)} fusion(s32[]{:T(128)S(6)} %select_n.181, bf16[512,6144]{1,0:T(8,128)(2,1)S(1)} %constant_dynamic-update-slice_fusion.8), kind=kLoop, calls=%fused_computation.8 | loop fusion | flops 12582912 | bytes 12582916 | tf_op jit(solution)/shard_map/jit(_roll_dynamic)/concatenate | solution.py:154
  280.6 5.4 %convolution_convert_fusion = bf16[512,6144]{1,0:T(8,128)(2,1)} fusion(bf16[1,512,6144]{2,1,0:T(8,128)(2,1)S(1)} %bitcast.144, f32[512,512]{1,0:T(8,128)S(1)} %fusion.4, f32[512,512]{1,0:T(8,128)S(1)} %fusion.8), kind=kOutput, calls=%fused_computation.5 | convolution fusion | flops 3225944064 | bytes 14680064 | tf_op jit(solution)/shard_map/dot_general | solution.py:163
  286.0 3.6 all-to-all-start.3
  289.8 39.3 %reduce-scatter.5.cloned.1.call-done = bf16[64,6144]{1,0:T(8,128)(2,1)} async-done(((bf16[512,6144]{1,0:T(8,128)(2,1)}), bf16[64,6144]{1,0:T(8,128)(2,1)}) %reduce-scatter.5.cloned.1.call-update) | async-done | bytes 786448 | tf_op jit(solution)/shard_map/reduce_scatter | solution.py:164
  329.1 6.7 %all-to-all-start.4 = ((bf16[8,8,6144]{2,1,0:T(8,128)(2,1)}), bf16[8,8,6144]{2,1,0:T(8,128)(2,1)}, u32[]{:S(2)}, u32[]{:S(2)}) async-start(bf16[8,8,6144]{2,1,0:T(8,128)(2,1)} %bitcast.126), calls=%async_computation.6 | async-start | bytes 1572864 | tf_op jit(solution)/shard_map/all_to_all | solution.py:166
  336.1 13.6 %all-to-all-done.4 = bf16[8,8,6144]{2,1,0:T(8,128)(2,1)} async-done(((bf16[8,8,6144]{2,1,0:T(8,128)(2,1)}), bf16[8,8,6144]{2,1,0:T(8,128)(2,1)}, u32[]{:S(2)}, u32[]{:S(2)}) %all-to-all-start.4) | async-done | bytes 786464 | tf_op jit(solution)/shard_map/all_to_all | solution.py:166
  354.4 9.6 %collective-permute-done.23 = bf16[32,6144]{1,0:T(8,128)(2,1)S(1)} collective-permute-done((bf16[32,6144]{1,0:T(8,128)(2,1)S(1)}, bf16[32,6144]{1,0:T(8,128)(2,1)S(1)}, u32[]{:S(2)}, u32[]{:S(2)}) %collective-permute-start.23) | collective-permute-done | bytes 393248 | tf_op jit(solution)/shard_map/ppermute | solution.py:182
  (186 shorter events, 69.7 us)
Async XLA Ops:
  8.7 23.0 %collective-permute-start = (bf16[520,384]{0,1:T(8,128)(2,1)S(1)}, bf16[520,384]{0,1:T(8,128)(2,1)S(1)}, u32[]{:S(2)}, u32[]{:S(2)}) collective-permute-start(bf16[520,384]{0,1:T(8,128)(2,1)S(1)} %pad_maximum_fusion.1), channel_id=1, source_target_pairs={{0,32},{16,48},{32,64},{48,80},{64,96},{80,112},{96,0},{112,16},{1... | collective-permute-start | bytes 1198088 | tf_op jit(solution)/shard_map/ppermute | solution.py:74
  10.7 21.1 %collective-permute-start.1 = (bf16[520,384]{0,1:T(8,128)(2,1)S(1)}, bf16[520,384]{0,1:T(8,128)(2,1)S(1)}, u32[]{:S(2)}, u32[]{:S(2)}) collective-permute-start(bf16[520,384]{0,1:T(8,128)(2,1)S(1)} %pad_maximum_fusion.1), channel_id=1, source_target_pairs={{0,64},{16,80},{32,96},{48,112},{64,0},{80,16},{96,32},{112,48},{1... | collective-permute-start | bytes 1198088 | tf_op jit(solution)/shard_map/ppermute | solution.py:74
  11.8 23.2 %collective-permute-start.2 = (bf16[520,384]{0,1:T(8,128)(2,1)S(1)}, bf16[520,384]{0,1:T(8,128)(2,1)S(1)}, u32[]{:S(2)}, u32[]{:S(2)}) collective-permute-start(bf16[520,384]{0,1:T(8,128)(2,1)S(1)} %pad_maximum_fusion.1), channel_id=1, source_target_pairs={{0,96},{16,112},{32,0},{48,16},{64,32},{80,48},{96,64},{112,80},{1... | collective-permute-start | bytes 1198088 | tf_op jit(solution)/shard_map/ppermute | solution.py:74
  14.3 20.8 %collective-permute-start.3 = (bf16[520,384]{0,1:T(8,128)(2,1)S(1)}, bf16[520,384]{0,1:T(8,128)(2,1)S(1)}, u32[]{:S(2)}, u32[]{:S(2)}) collective-permute-start(bf16[520,384]{0,1:T(8,128)(2,1)S(1)} %pad_maximum_fusion.1), channel_id=1, source_target_pairs={{0,16},{16,0},{32,48},{48,32},{64,80},{80,64},{96,112},{112,96},{1... | collective-permute-start | bytes 1198088 | tf_op jit(solution)/shard_map/ppermute | solution.py:76
  45.0 53.7 %all-to-all-start = ((bf16[16,16,6144]{2,1,0:T(8,128)(2,1)}), bf16[16,16,6144]{2,1,0:T(8,128)(2,1)S(1)}, u32[]{:S(2)}, u32[]{:S(2)}) async-start(bf16[16,16,6144]{2,1,0:T(8,128)(2,1)} %bitcast.116), calls=%async_computation | async-start | bytes 6291456 | tf_op jit(solution)/shard_map/all_to_all | solution.py:110
  52.1 233.9 %reduce-scatter.3.cloned.1.call-start = ((), (), s32[]{:S(2)}) async-start(), calls=%async_computation.7 | async-start | bytes 7077888 | tf_op jit(solution)/shard_map/reduce_scatter | solution.py:164
  126.4 11.4 %collective-permute-start.8 = (bf16[64,6144]{1,0:T(8,128)(2,1)S(1)}, bf16[64,6144]{1,0:T(8,128)(2,1)S(1)}, u32[]{:S(2)}, u32[]{:S(2)}) collective-permute-start(bf16[64,6144]{1,0:T(8,128)(2,1)S(1)} %bitcast.122), channel_id=1, source_target_pairs={{0,16},{16,32},{32,48},{48,64},{64,80},{80,96},{96,112},{112,0},{1... | collective-permute-start | bytes 2359304 | tf_op jit(solution)/shard_map/ppermute | solution.py:150
  137.9 11.4 %collective-permute-start.9 = (bf16[64,6144]{1,0:T(8,128)(2,1)S(1)}, bf16[64,6144]{1,0:T(8,128)(2,1)S(1)}, u32[]{:S(2)}, u32[]{:S(2)}) collective-permute-start(bf16[64,6144]{1,0:T(8,128)(2,1)S(1)} %collective-permute-done.8), channel_id=1, source_target_pairs={{0,16},{16,32},{32,48},{48,64},{64,80},{80,96},{96,112},{112,0},{1... | collective-permute-start | bytes 2359304 | tf_op jit(solution)/shard_map/ppermute | solution.py:150
  137.9 29.4 %collective-permute-start.12 = (bf16[64,6144]{1,0:T(8,128)(2,1)S(1)}, bf16[64,6144]{1,0:T(8,128)(2,1)}, u32[]{:S(2)}, u32[]{:S(2)}) collective-permute-start(bf16[64,6144]{1,0:T(8,128)(2,1)S(1)} %bitcast.123), channel_id=1, source_target_pairs={{0,112},{16,0},{32,16},{48,32},{64,48},{80,64},{96,80},{112,96},{1... | collective-permute-start | bytes 2359304 | tf_op jit(solution)/shard_map/ppermute | solution.py:152
  149.3 19.7 %collective-permute-start.10 = (bf16[64,6144]{1,0:T(8,128)(2,1)S(1)}, bf16[64,6144]{1,0:T(8,128)(2,1)}, u32[]{:S(2)}, u32[]{:S(2)}) collective-permute-start(bf16[64,6144]{1,0:T(8,128)(2,1)S(1)} %collective-permute-done.9), channel_id=1, source_target_pairs={{0,16},{16,32},{32,48},{48,64},{64,80},{80,96},{96,112},{112,0},{1... | collective-permute-start | bytes 2359304 | tf_op jit(solution)/shard_map/ppermute | solution.py:150
  167.2 11.4 %collective-permute-start.15 = (bf16[64,6144]{1,0:T(8,128)(2,1)S(1)}, bf16[64,6144]{1,0:T(8,128)(2,1)S(1)}, u32[]{:S(2)}, u32[]{:S(2)}) collective-permute-start(bf16[64,6144]{1,0:T(8,128)(2,1)S(1)} %bitcast.120), channel_id=1, source_target_pairs={{0,16},{16,32},{32,48},{48,64},{64,80},{80,96},{96,112},{112,0},{1... | collective-permute-start | bytes 2359304 | tf_op jit(solution)/shard_map/ppermute | solution.py:150
  167.2 11.6 %collective-permute-start.13 = (bf16[64,6144]{1,0:T(8,128)(2,1)}, bf16[64,6144]{1,0:T(8,128)(2,1)}, u32[]{:S(2)}, u32[]{:S(2)}) collective-permute-start(bf16[64,6144]{1,0:T(8,128)(2,1)} %collective-permute-done.12), channel_id=1, source_target_pairs={{0,112},{16,0},{32,16},{48,32},{64,48},{80,64},{96,80},{112,96},{1... | collective-permute-start | bytes 2359304 | tf_op jit(solution)/shard_map/ppermute | solution.py:152
  169.0 18.2 %collective-permute-start.11 = (bf16[64,6144]{1,0:T(8,128)(2,1)}, bf16[64,6144]{1,0:T(8,128)(2,1)}, u32[]{:S(2)}, u32[]{:S(2)}) collective-permute-start(bf16[64,6144]{1,0:T(8,128)(2,1)} %collective-permute-done.10), channel_id=1, source_target_pairs={{0,16},{16,32},{32,48},{48,64},{64,80},{80,96},{96,112},{112,0},{1... | collective-permute-start | bytes 2359304 | tf_op jit(solution)/shard_map/ppermute | solution.py:150
  178.7 35.2 %collective-permute-start.16 = (bf16[64,6144]{1,0:T(8,128)(2,1)S(1)}, bf16[64,6144]{1,0:T(8,128)(2,1)}, u32[]{:S(2)}, u32[]{:S(2)}) collective-permute-start(bf16[64,6144]{1,0:T(8,128)(2,1)S(1)} %collective-permute-done.15), channel_id=1, source_target_pairs={{0,16},{16,32},{32,48},{48,64},{64,80},{80,96},{96,112},{112,0},{1... | collective-permute-start | bytes 2359304 | tf_op jit(solution)/shard_map/ppermute | solution.py:150
  178.8 15.7 %collective-permute-start.14 = (bf16[64,6144]{1,0:T(8,128)(2,1)}, bf16[64,6144]{1,0:T(8,128)(2,1)S(1)}, u32[]{:S(2)}, u32[]{:S(2)}) collective-permute-start(bf16[64,6144]{1,0:T(8,128)(2,1)} %collective-permute-done.13), channel_id=1, source_target_pairs={{0,112},{16,0},{32,16},{48,32},{64,48},{80,64},{96,80},{112,96},{1... | collective-permute-start | bytes 2359304 | tf_op jit(solution)/shard_map/ppermute | solution.py:152
  213.7 115.3 %reduce-scatter.5.cloned.1.call-start = ((), (), s32[]{:S(2)}) async-start(), calls=%async_computation.8 | async-start | bytes 7077888 | tf_op jit(solution)/shard_map/reduce_scatter | solution.py:164
  213.8 12.4 %collective-permute-start.19 = (bf16[64,6144]{1,0:T(8,128)(2,1)S(1)}, bf16[64,6144]{1,0:T(8,128)(2,1)S(1)}, u32[]{:S(2)}, u32[]{:S(2)}) collective-permute-start(bf16[64,6144]{1,0:T(8,128)(2,1)S(1)} %bitcast.121), channel_id=1, source_target_pairs={{0,112},{16,0},{32,16},{48,32},{64,48},{80,64},{96,80},{112,96},{1... | collective-permute-start | bytes 2359304 | tf_op jit(solution)/shard_map/ppermute | solution.py:152
  213.8 18.3 %collective-permute-start.17 = (bf16[64,6144]{1,0:T(8,128)(2,1)}, bf16[64,6144]{1,0:T(8,128)(2,1)S(1)}, u32[]{:S(2)}, u32[]{:S(2)}) collective-permute-start(bf16[64,6144]{1,0:T(8,128)(2,1)} %collective-permute-done.16), channel_id=1, source_target_pairs={{0,16},{16,32},{32,48},{48,64},{64,80},{80,96},{96,112},{112,0},{1... | collective-permute-start | bytes 2359304 | tf_op jit(solution)/shard_map/ppermute | solution.py:150
  226.2 20.3 %collective-permute-start.20 = (bf16[64,6144]{1,0:T(8,128)(2,1)S(1)}, bf16[64,6144]{1,0:T(8,128)(2,1)S(1)}, u32[]{:S(2)}, u32[]{:S(2)}) collective-permute-start(bf16[64,6144]{1,0:T(8,128)(2,1)S(1)} %collective-permute-done.19), channel_id=1, source_target_pairs={{0,112},{16,0},{32,16},{48,32},{64,48},{80,64},{96,80},{112,96},{1... | collective-permute-start | bytes 2359304 | tf_op jit(solution)/shard_map/ppermute | solution.py:152
  232.1 19.9 %collective-permute-start.18 = (bf16[64,6144]{1,0:T(8,128)(2,1)S(1)}, bf16[64,6144]{1,0:T(8,128)(2,1)S(1)}, u32[]{:S(2)}, u32[]{:S(2)}) collective-permute-start(bf16[64,6144]{1,0:T(8,128)(2,1)S(1)} %collective-permute-done.17), channel_id=1, source_target_pairs={{0,16},{16,32},{32,48},{48,64},{64,80},{80,96},{96,112},{112,0},{1... | collective-permute-start | bytes 2359304 | tf_op jit(solution)/shard_map/ppermute | solution.py:150
  246.6 20.3 %collective-permute-start.21 = (bf16[64,6144]{1,0:T(8,128)(2,1)S(1)}, bf16[64,6144]{1,0:T(8,128)(2,1)S(1)}, u32[]{:S(2)}, u32[]{:S(2)}) collective-permute-start(bf16[64,6144]{1,0:T(8,128)(2,1)S(1)} %collective-permute-done.20), channel_id=1, source_target_pairs={{0,112},{16,0},{32,16},{48,32},{64,48},{80,64},{96,80},{112,96},{1... | collective-permute-start | bytes 2359304 | tf_op jit(solution)/shard_map/ppermute | solution.py:152
  248.9 24.8 %collective-permute-start.22 = (f32[16,6144]{1,0:T(8,128)S(1)}, f32[16,6144]{1,0:T(8,128)S(1)}, u32[]{:S(2)}, u32[]{:S(2)}) collective-permute-start(f32[16,6144]{1,0:T(8,128)S(1)} %copy-done.2), channel_id=1, source_target_pairs={{0,1},{1,0},{2,3},{3,2},{4,5},{5,4},{6,7},{7,6},{8,9},{9,8},{10,11... | collective-permute-start | bytes 1179656 | tf_op jit(solution)/shard_map/ppermute | solution.py:157
  286.0 43.1 %all-to-all-start.3 = ((bf16[8,8,6144]{2,1,0:T(8,128)(2,1)}), bf16[8,8,6144]{2,1,0:T(8,128)(2,1)S(1)}, u32[]{:S(2)}, u32[]{:S(2)}) async-start(bf16[8,8,6144]{2,1,0:T(8,128)(2,1)} %bitcast.125), calls=%async_computation.4 | async-start | bytes 1572864 | tf_op jit(solution)/shard_map/all_to_all | solution.py:166
  329.1 20.7 %all-to-all-start.4 = ((bf16[8,8,6144]{2,1,0:T(8,128)(2,1)}), bf16[8,8,6144]{2,1,0:T(8,128)(2,1)}, u32[]{:S(2)}, u32[]{:S(2)}) async-start(bf16[8,8,6144]{2,1,0:T(8,128)(2,1)} %bitcast.126), calls=%async_computation.6 | async-start | bytes 1572864 | tf_op jit(solution)/shard_map/all_to_all | solution.py:166
  (30 other events, 629.3 us)
Sparse Core Ops, SparseCore 0:
  213.9 57.0 reduce-scatter.2
  286.1 42.9 reduce-scatter.4
